TPU v7x, 32 devices: a whole 2x2x4 slice. The times are simulated.
32 devices in a mesh: blk: 16 (over z, y, core), rep: 2 (over x).
Axes of the slice: x: 2, y: 2, z: 4, core: 2. Of those that a mesh axis runs over, the one named last changes fastest.
Arguments:
- qm_pos: float32 [3, 2048], P(None, 'blk'), may hold values from -4 to 4
- species: int32 [2048], P('blk'), may hold values from 0 to 7
- qm_count: int32 [16], P('blk'), may hold values from 64 to 128, as said below
- ghost_owner: int32 [2048, 4], P('blk'), may hold values from 0 to 15, all different within a row; in each aligned block of 128 rows (0 to 127, 128 to 255, ...) at most 64 rows name the same one
- ghost_slot: int32 [2048, 4], P('blk'), may hold values from 0 to 127
- mm_pos: float32 [3, 16384], P(None, ('blk', 'rep')), may hold values from -4 to 4
- mm_charge: float32 [16384], P(('blk', 'rep')), may hold values from -6 to 6
- species_table: bfloat16 [8, 128], replicated, may hold values from -6 to 6
- potential_gain: float32 [128], replicated, may hold values from -8 to 8
- message_weight: bfloat16 [128, 128], replicated, may hold values from -0.25 to 0.25
- hidden_weight: bfloat16 [128, 256], replicated, may hold values from -0.5 to 0.5
- energy_readout: float32 [256], replicated, may hold values from -0.375 to 0.375
- charge_readout: float32 [256], replicated, may hold values from -0.375 to 0.375
Outputs:
- atom_energy: float32 [2048], P('blk')
- qm_force: float32 [3, 2048], P(None, 'blk')
- mm_force: float32 [3, 16384], P(None, ('blk', 'rep'))
Inputs may be any that keep to these rules, and one draw needn't show every extreme that they name: `qm_count`: some block holds exactly 128 live atoms. `ghost_owner`: each row names 4 different blocks; among the rows of one device no block is named more than 64 times, and some block exactly 64 times.
All inputs are finite; a program needn't handle non-finite values.
Results may differ from a plain program's by a relative error of at most 0.0055.
Values may be sent and summed in bfloat16 or wider, within the bound.
No kernel may reach another device: no remote copies, remote signals or barrier semaphores. Data moves between devices by JAX's collectives and lax.ppermute only.
A program may use at most 64 MiB of HBM per device.

v0:
```python
import math
import jax
import jax.numpy as jnp
from jax import lax
from jax.sharding import PartitionSpec as P

SOFTEN = 0.25


def pair_parts(qm_places, mm_places):
    offset = qm_places[:, :, None] - mm_places[:, None, :]
    inverse = lax.rsqrt(jnp.sum(offset * offset, axis=0) + SOFTEN)
    return (offset, inverse)


def split_columns(stacked, limit):
    stride = math.gcd(stacked.shape[1], limit)
    shaped = stacked.reshape(stacked.shape[0], stacked.shape[1] // stride, stride)
    return jnp.transpose(shaped, (1, 0, 2))


def potential_from(qm_places, mm_stack):

    def potential_advance(running, columns):
        offset, inverse = pair_parts(qm_places, columns[:3])
        return (running + jnp.sum(inverse * columns[3][None, :], axis=1), None)

    result, _ = lax.scan(
        potential_advance,
        jnp.zeros((qm_places.shape[1],), jnp.float32),
        split_columns(mm_stack, 512),
    )
    return result


def on_device(
    qm_pos,
    species,
    qm_count,
    ghost_owner,
    ghost_slot,
    mm_pos,
    mm_charge,
    species_table,
    potential_gain,
    message_weight,
    hidden_weight,
    energy_readout,
    charge_readout,
):
    atom_rows = qm_pos.shape[1]
    blocks = lax.axis_size("blk")
    neighbours = ghost_owner.shape[1]
    channels = species_table.shape[1]
    capacity = 2 * atom_rows * neighbours // blocks
    coupling = float(mm_pos.shape[1] * blocks * lax.axis_size("rep")) ** (-0.5)
    mm_stack = jnp.concatenate([mm_pos, mm_charge[None, :]], axis=0)
    partial_sum = potential_from(qm_pos, lax.all_gather(mm_stack, "blk", axis=1, tiled=True))
    potential = lax.psum(partial_sum, "rep") * coupling
    live = (jnp.arange(atom_rows) < qm_count[0]).astype(jnp.float32)
    picks = (species[:, None] == jnp.arange(species_table.shape[0])[None, :]).astype(jnp.bfloat16)
    base = jnp.dot(picks, species_table, preferred_element_type=jnp.float32)
    start = (live[:, None] * (base + potential[:, None] * potential_gain[None, :])).astype(
        jnp.bfloat16
    )
    owners = ghost_owner.reshape(-1)
    slots = ghost_slot.reshape(-1)
    hits = (owners[:, None] == jnp.arange(blocks)[None, :]).astype(jnp.int32)
    ranks = jnp.sum((jnp.cumsum(hits, axis=0) - hits) * hits, axis=1)
    request = jnp.zeros((blocks, capacity), jnp.int32).at[owners, ranks].set(slots)
    wanted = lax.all_to_all(request, "blk", split_axis=0, concat_axis=0, tiled=True)
    outgoing = jnp.take(start, wanted, axis=0)
    arrived = lax.all_to_all(outgoing, "blk", split_axis=0, concat_axis=0, tiled=True)
    ghosts = arrived[owners, ranks]
    neighbour = jnp.sum(
        ghosts.reshape(atom_rows, neighbours, channels).astype(jnp.float32), axis=1
    ).astype(jnp.bfloat16)
    mixed = start.astype(jnp.float32) + jnp.dot(
        neighbour, message_weight, preferred_element_type=jnp.float32
    )
    before = jnp.dot(mixed.astype(jnp.bfloat16), hidden_weight, preferred_element_type=jnp.float32)
    sigma = jax.nn.sigmoid(before)
    active = before * sigma
    energy_part = live * jnp.sum(active * energy_readout[None, :], axis=1)
    charge_part = live * jnp.sum(active * charge_readout[None, :], axis=1)
    atom_energy = energy_part + charge_part * potential
    back_active = live[:, None] * (
        energy_readout[None, :] + potential[:, None] * charge_readout[None, :]
    )
    back_before = (back_active * sigma * (1.0 + before * (1.0 - sigma))).astype(jnp.bfloat16)
    back_mixed = jnp.dot(back_before, hidden_weight.T, preferred_element_type=jnp.float32)
    back_sum = jnp.dot(
        back_mixed.astype(jnp.bfloat16), message_weight.T, preferred_element_type=jnp.float32
    ).astype(jnp.bfloat16)
    outgoing_grads = (
        jnp.zeros((blocks, capacity, channels), jnp.bfloat16)
        .at[owners, ranks]
        .set(jnp.repeat(back_sum, neighbours, axis=0))
    )
    returned = lax.all_to_all(outgoing_grads, "blk", split_axis=0, concat_axis=0, tiled=True)
    picks_back = (wanted.reshape(-1)[:, None] == jnp.arange(atom_rows)[None, :]).astype(
        jnp.bfloat16
    )
    collected = jnp.einsum(
        "ra,rf->af",
        picks_back,
        returned.reshape(blocks * capacity, channels),
        preferred_element_type=jnp.float32,
    )
    back_start = back_mixed + collected
    effective = charge_part + live * jnp.sum(back_start * potential_gain[None, :], axis=1)
    qm_stack = jnp.concatenate([qm_pos, effective[None, :]], axis=0)
    portion = lax.all_gather(qm_stack, "blk", axis=1, tiled=True)
    mm_running = jnp.zeros((3, mm_pos.shape[1]), jnp.float32)

    def add_advance(running, group):
        offset, inverse = pair_parts(group[:3], mm_pos)
        weight = inverse * inverse * inverse * mm_charge[None, :]
        pull = jnp.sum(offset * weight[None], axis=2) * group[3][None, :]
        running = running - jnp.sum(offset * (weight * group[3][:, None])[None], axis=1)
        return (running, pull)

    mm_running, pulls = lax.scan(add_advance, mm_running, split_columns(portion, 512))
    block_terms = jnp.transpose(pulls, (1, 0, 2)).reshape(3, portion.shape[1])
    qm_terms = block_terms
    mm_sum, qm_terms = (mm_running, qm_terms)
    block_force = lax.psum_scatter(qm_terms, "blk", scatter_dimension=1, tiled=True)
    qm_force = lax.psum(block_force, "rep") * coupling
    return (atom_energy, qm_force, mm_sum * coupling)


def solution(mesh):
    placed = (
        P(None, "blk"),
        P("blk"),
        P("blk"),
        P("blk", None),
        P("blk", None),
        P(None, ("blk", "rep")),
        P(("blk", "rep")),
        P(),
        P(),
        P(),
        P(),
        P(),
        P(),
    )
    return jax.shard_map(
        on_device,
        mesh=mesh,
        in_specs=placed,
        out_specs=(P("blk"), P(None, "blk"), P(None, ("blk", "rep"))),
        check_vma=False,
    )
```

profile of v0, /device:TPU:0, one launch (start us, length us, event | category | flops | bytes accessed | tf_op | source)
XLA Modules:
  0.0 304.6 jit_solution(3147633748383444944)
XLA Ops:
  7.2 0.8 copy.36
  8.3 1.2 reduce-window.6
  9.5 0.2 slice_reduce_fusion
  9.8 0.8 copy.40
  10.8 0.6 broadcast_in_dim.31
  11.4 69.8 %scatter_fusion = s32[16,64]{1,0:T(8,128)} fusion(s32[16,64]{1,0:T(8,128)} %broadcast_in_dim.31, s32[512]{0:T(512)S(1)} %bitcast.80, s32[512]{0:T(512)S(1)} %reshape.281), kind=kCustom, calls=%fused_computation.2 | custom fusion | bytes 10240 | tf_op jit(solution)/shard_map/scatter | solution.py:70
  81.2 7.4 %all-to-all-start = ((s32[16,1,64]{2,1,0:T(1,128)}), s32[16,1,64]{2,1,0:T(1,128)S(1)}, u32[]{:S(2)}, u32[]{:S(2)}) async-start(s32[16,1,64]{2,1,0:T(1,128)} %bitcast.8), calls=%async_computation | async-start | bytes 16384 | tf_op jit(solution)/shard_map/all_to_all | solution.py:71
  88.6 22.1 %all_gather.6 = f32[4,8192]{1,0:T(4,128)S(1)} all-gather(f32[4,512]{1,0:T(4,128)S(1)} %pad_maximum_fusion), channel_id=1, replica_groups=mesh['blk'=16,'rep'=2] {'blk'}, dimensions={1}, use_global_device_ids=true | all-gather | bytes 139264 | tf_op jit(solution)/shard_map/all_gather | solution.py:58
  110.7 5.4 %while.24 = (s32[]{:T(128)}, f32[128]{0:T(128)S(1)}, f32[3,128]{1,0:T(4,128)S(1)}, f32[16,4,512]{2,1,0:T(4,128)S(1)}, s32[]{:T(128)}, /*index=5*/s32[]{:T(128)}, s32[]{}) while((s32[]{:T(128)}, f32[128]{0:T(128)S(1)}, f32[3,128]{1,0:T(4,128)S(1)}, f32[16,4,512]{2,1,0:T(4,128)S(1)}, s32[]{:T(128)}, /*index=5*/s32[]{:T(128)}, ...), condition=%wide.region_3.4_spmd.clone, body=%wide.region_0.3_spmd.clone.sunk | while | flops 721028 | bytes 552567 | solution.py:28
  110.7 0.1 multiply_reduce_fusion.6
  116.1 4.9 %psum.14 = f32[128]{0:T(128)S(1)} all-reduce(f32[128]{0:T(128)S(1)} %get-tuple-element.58), channel_id=1, replica_groups=mesh['blk'=16,'rep'=2] {'rep'}, use_global_device_ids=true, to_apply=%region_4.5 | all-reduce | flops 128 | bytes 1024 | tf_op jit(solution)/shard_map/psum | solution.py:59
  121.7 0.2 fusion.8
  122.1 3.2 %gather_fusion = bf16[1024,128]{1,0:T(8,128)(2,1)S(1)} fusion(bf16[128,128]{1,0:T(8,128)(2,1)S(1)} %fusion.8, s32[1024]{0:T(1024)S(1)} %broadcast_clamp_fusion), kind=kCustom, calls=%fused_computation | custom fusion | bytes 528384 | tf_op jit(solution)/shard_map/jit(_take)/gather | solution.py:72
  125.3 0.2 broadcast_select_fusion.1
  125.5 12.8 %all_to_all.25 = bf16[16,64,128]{2,1,0:T(8,128)(2,1)S(1)} all-to-all(bf16[16,64,128]{2,1,0:T(8,128)(2,1)S(1)} %broadcast_select_fusion.1), channel_id=1, replica_groups=mesh['blk'=16,'rep'=2] {'blk'}, dimensions={0} | all-to-all | bytes 524288 | tf_op jit(solution)/shard_map/all_to_all | solution.py:73
  138.3 3.2 %gather_fusion.1 = bf16[512,128]{1,0:T(8,128)(2,1)S(1)} fusion(bf16[16,64,128]{2,1,0:T(8,128)(2,1)S(1)} %all_to_all.25, s32[512]{0:T(512)S(1)} %bitcast.82), kind=kCustom, calls=%fused_computation.1 | custom fusion | bytes 266240 | tf_op jit(solution)/shard_map/gather | solution.py:74
  141.5 0.2 reduce_sum.103
  141.7 0.4 multiply_reduce_fusion.3
  142.1 0.2 fusion.15
  142.3 0.2 convolution_convert_fusion
  142.6 0.7 broadcast_in_dim.37
  143.3 52.6 %scatter_fusion.1 = bf16[16,64,128]{2,1,0:T(8,128)(2,1)} fusion(bf16[16,64,128]{2,1,0:T(8,128)(2,1)} %broadcast_in_dim.37, s32[512]{0:T(512)S(1)} %bitcast.81, bf16[512,128]{1,0:T(8,128)(2,1)S(1)} %bitcast.85), kind=kCustom, calls=%fused_computation.3 | custom fusion | bytes 397312 | tf_op jit(solution)/shard_map/scatter | solution.py:98
  195.9 3.5 %all-to-all-start.2 = ((bf16[16,64,128]{2,1,0:T(8,128)(2,1)}), bf16[16,64,128]{2,1,0:T(8,128)(2,1)S(1)}, u32[]{:S(2)}, u32[]{:S(2)}) async-start(bf16[16,64,128]{2,1,0:T(8,128)(2,1)} %scatter_fusion.1), calls=%async_computation.2 | async-start | bytes 524288 | tf_op jit(solution)/shard_map/all_to_all | solution.py:100
  199.5 0.5 broadcast.292
  200.0 0.7 reduce.6
  200.8 0.5 multiply_add_fusion
  201.3 8.1 %all-to-all-done.2 = bf16[16,64,128]{2,1,0:T(8,128)(2,1)S(1)} async-done(((bf16[16,64,128]{2,1,0:T(8,128)(2,1)}), bf16[16,64,128]{2,1,0:T(8,128)(2,1)S(1)}, u32[]{:S(2)}, u32[]{:S(2)}) %all-to-all-start.2) | async-done | bytes 262176 | tf_op jit(solution)/shard_map/all_to_all | solution.py:100
  209.4 0.6 fusion.10
  210.0 18.8 %all_gather.7 = f32[4,2048]{1,0:T(4,128)S(1)} all-gather(f32[4,128]{1,0:T(4,128)S(1)} %pad_maximum_fusion.1), channel_id=1, replica_groups=mesh['blk'=16,'rep'=2] {'blk'}, dimensions={1}, use_global_device_ids=true | all-gather | bytes 34816 | tf_op jit(solution)/shard_map/all_gather | solution.py:113
  228.8 6.3 %while.25 = (s32[]{:T(128)}, f32[3,512]{1,0:T(4,128)S(1)}, f32[4,3,512]{2,1,0:T(4,128)S(1)}, f32[4,4,512]{2,1,0:T(4,128)S(1)}, f32[3,512]{1,0:T(4,128)S(1)}, /*index=5*/f32[512]{0:T(512)S(1)}, s32[]{:T(128)}, s32[]{:T(128)}, s32[]{}) while((s32[]{:T(128)}, f32[3,512]{1,0:T(4,128)S(1)}, f32[4,3,512]{2,1,0:T(4,128)S(1)}, ...), condition=%wide.region_18.19_spmd.clone, body=%wide.region_14.18_spmd.clone.sunk | while | flops 7341572 | bytes 6385803 | solution.py:123
  228.8 0.4 fusion.39
  229.1 0.2 broadcast_multiply_fusion.5
  229.4 0.9 fusion.40
  230.4 0.4 fusion.39
  230.7 0.2 broadcast_multiply_fusion.5
  231.0 0.9 fusion.40
  232.0 0.4 fusion.39
  232.3 0.2 broadcast_multiply_fusion.5
  232.5 0.9 fusion.40
  233.5 0.4 fusion.39
  233.9 0.2 broadcast_multiply_fusion.5
  234.1 0.9 fusion.40
  235.1 1.4 copy.46
  236.5 0.6 broadcast_multiply_fusion.1
  237.1 54.2 %reduce-scatter.4.cloned.1.call-done = f32[128,3]{1,0:T(8,128)} async-done(((f32[2048,3]{1,0:T(8,128)}), f32[128,3]{1,0:T(8,128)}) %reduce-scatter.4.cloned.1.call-update) | async-done | bytes 1552
  291.3 0.9 copy.47
  292.2 4.9 %psum.15 = f32[3,128]{1,0:T(4,128)S(1)} all-reduce(f32[3,128]{1,0:T(4,128)S(1)} %copy.47), channel_id=1, replica_groups=mesh['blk'=16,'rep'=2] {'rep'}, use_global_device_ids=true, to_apply=%region_20.21 | all-reduce | flops 384 | bytes 3072 | tf_op jit(solution)/shard_map/psum | solution.py:128
  297.2 0.6 broadcast_multiply_fusion.2
  (142 shorter events, 5.8 us)
Async XLA Ops:
  7.2 134.5 %copy-start = (bf16[128,256]{1,0:T(8,128)(2,1)S(1)}, bf16[128,256]{1,0:T(8,128)(2,1)}, u32[]{:S(2)}) copy-start(bf16[128,256]{1,0:T(8,128)(2,1)} %param.27) | copy-start | bytes 196612
  11.4 77.2 %copy-start.1 = (f32[3,512]{1,0:T(4,128)S(1)}, f32[3,512]{1,0:T(4,128)}, u32[]{:S(2)}) copy-start(f32[3,512]{1,0:T(4,128)} %param.22) | copy-start | bytes 18436
  11.4 77.2 %copy-start.3 = (f32[512]{0:T(512)S(1)}, f32[512]{0:T(512)}, u32[]{:S(2)}) copy-start(f32[512]{0:T(512)} %param.23) | copy-start | bytes 6148
  11.4 99.3 %copy-start.2 = (f32[3,128]{1,0:T(4,128)S(1)}, f32[3,128]{1,0:T(4,128)}, u32[]{:S(2)}) copy-start(f32[3,128]{1,0:T(4,128)} %param.17) | copy-start | bytes 4612
  81.2 40.8 %all-to-all-start = ((s32[16,1,64]{2,1,0:T(1,128)}), s32[16,1,64]{2,1,0:T(1,128)S(1)}, u32[]{:S(2)}, u32[]{:S(2)}) async-start(s32[16,1,64]{2,1,0:T(1,128)} %bitcast.8), calls=%async_computation | async-start | bytes 16384 | tf_op jit(solution)/shard_map/all_to_all | solution.py:71
  110.7 11.0 %copy-start.5 = (bf16[8,128]{1,0:T(8,128)(2,1)S(1)}, bf16[8,128]{1,0:T(8,128)(2,1)}, u32[]{:S(2)}) copy-start(bf16[8,128]{1,0:T(8,128)(2,1)} %param.24) | copy-start | bytes 6148
  110.7 11.0 %copy-start.8 = (s32[128]{0:T(128)S(1)}, s32[128]{0:T(128)}, u32[]{:S(2)}) copy-start(s32[128]{0:T(128)} %param.18) | copy-start | bytes 1540
  110.7 11.0 %copy-start.9 = (f32[128]{0:T(128)S(1)}, f32[128]{0:T(128)}, u32[]{:S(2)}) copy-start(f32[128]{0:T(128)} %param.25) | copy-start | bytes 1540
  125.5 16.2 %copy-start.4 = (bf16[128,128]{1,0:T(8,128)(2,1)S(1)}, bf16[128,128]{1,0:T(8,128)(2,1)}, u32[]{:S(2)}) copy-start(bf16[128,128]{1,0:T(8,128)(2,1)} %param.26) | copy-start | bytes 98308
  125.5 16.2 %copy-start.6 = (f32[256]{0:T(256)S(1)}, f32[256]{0:T(256)}, u32[]{:S(2)}) copy-start(f32[256]{0:T(256)} %param.28) | copy-start | bytes 3076
  125.5 16.2 %copy-start.7 = (f32[256]{0:T(256)S(1)}, f32[256]{0:T(256)}, u32[]{:S(2)}) copy-start(f32[256]{0:T(256)} %param.29) | copy-start | bytes 3076
  195.9 13.5 %all-to-all-start.2 = ((bf16[16,64,128]{2,1,0:T(8,128)(2,1)}), bf16[16,64,128]{2,1,0:T(8,128)(2,1)S(1)}, u32[]{:S(2)}, u32[]{:S(2)}) async-start(bf16[16,64,128]{2,1,0:T(8,128)(2,1)} %scatter_fusion.1), calls=%async_computation.2 | async-start | bytes 524288 | tf_op jit(solution)/shard_map/all_to_all | solution.py:100
  199.4 91.9 %reduce-scatter.4.cloned.1.call-start = ((), (), s32[]{:S(2)}) async-start(), calls=%async_computation.4 | async-start | bytes 1114112
Sparse Core Ops, SparseCore 0:
  236.6 54.6 reduce-scatter.3
where the time goes:
time: 307 us; the launch traced here: 305 us
  local copies, waits for them, and re-layouts  136 us (44%)
  blocking collectives  63.5 us (21%)
  waiting for transfers between devices  62.3 us (20%)
  between operations  15 us (5%)
  other arithmetic  14.6 us (5%)
  starting transfers between devices  11 us (4%)
    scatter x1, local copies, waits for them, and re-layouts, on_device(): jnp.zeros((blocks, capacity), jnp.int32).at[owners, ranks].set(slots)  69.8 us
    unnamed x2, waiting for transfers between devices  54.3 us
    scatter x1, local copies, waits for them, and re-layouts, on_device(): outgoing_grads = jnp.zeros((blocks, capacity, channels), jnp.bfloat16).at...  52.6 us
    all_gather x1, blocking collectives, on_device(): lax.all_gather(mm_stack, 'blk', axis=1, tiled=True)  22.1 us
    all_gather x1, blocking collectives, on_device(): portion = lax.all_gather(qm_stack, 'blk', axis=1, tiled=True)  18.8 us
    all_to_all x1, blocking collectives, on_device(): lax.all_to_all(outgoing, 'blk', split_axis=0, concat_axis=0, tiled=True)  12.8 us
    all_to_all x1, waiting for transfers between devices, on_device(): lax.all_to_all(outgoing_grads, 'blk', split_axis=0, concat_axis=0, tiled=...  8.06 us
    all_to_all x1, starting transfers between devices, on_device(): lax.all_to_all(request, 'blk', split_axis=0, concat_axis=0, tiled=True)  7.38 us
  transfers between devices with their start and end apart: 3, of which 2 were waited for; matrix products, arithmetic and copies ran while one was open for 2% of the time, Pallas kernels for 0%

commit v1 on v0

--- a/solution.py
+++ b/solution.py
@@ -5,6 +5,22 @@
 from jax.sharding import PartitionSpec as P
 
 SOFTEN = 0.25
+
+
+def exchange_in_pairs(x, axis, split, join):
+    ways, here = (lax.axis_size(axis), lax.axis_index(axis))
+    width = x.shape[split] // ways
+    shape = list(x.shape)
+    shape[split] = width
+    height = shape[join]
+    shape[join] = height * ways
+    full = jnp.zeros(shape, x.dtype)
+    for mask in range(ways):
+        part = lax.dynamic_slice_in_dim(x, (here ^ mask) * width, width, axis=split)
+        if mask:
+            part = lax.ppermute(part, axis, [(d, d ^ mask) for d in range(ways)])
+        full = lax.dynamic_update_slice_in_dim(full, part, (here ^ mask) * height, axis=join)
+    return full
 
 
 def pair_parts(qm_places, mm_places):
@@ -68,7 +84,7 @@
     hits = (owners[:, None] == jnp.arange(blocks)[None, :]).astype(jnp.int32)
     ranks = jnp.sum((jnp.cumsum(hits, axis=0) - hits) * hits, axis=1)
     request = jnp.zeros((blocks, capacity), jnp.int32).at[owners, ranks].set(slots)
-    wanted = lax.all_to_all(request, "blk", split_axis=0, concat_axis=0, tiled=True)
+    wanted = exchange_in_pairs(request, "blk", 0, 0)
     outgoing = jnp.take(start, wanted, axis=0)
     arrived = lax.all_to_all(outgoing, "blk", split_axis=0, concat_axis=0, tiled=True)
     ghosts = arrived[owners, ranks]

time: 307 us -> 281 us (0.915)
  local copies, waits for them, and re-layouts: 136 us -> 90.8 us
  starting transfers between devices: 11 us -> 24.7 us
  waiting for transfers between devices: 62.3 us -> 66.3 us
    scatter x1, local copies, waits for them, and re-layouts: 69.8 us -> 25.3 us  [on_device(): jnp.zeros((blocks, capacity), jnp.int32).at[owners, ranks].set(slots)]
    ppermute x0 -> x15, starting transfers between devices: none -> 21.1 us  [exchange_in_pairs(): part = lax.ppermute(part, axis, [(d, d ^ mask) for d in range(ways)])]
    all_to_all x1 -> x0, starting transfers between devices: 7.38 us -> none  [on_device(): lax.all_to_all(request, 'blk', split_axis=0, concat_axis=0, tiled=True)]
  transfers between devices with their start and end apart: 3 -> 17, of which waited for: 2 -> 3; matrix products, arithmetic and copies ran while one was open for 2% -> 2% of each run, Pallas kernels for 0% -> 0%
where the time goes in v1:
time: 281 us; the launch traced here: 280 us
  local copies, waits for them, and re-layouts  90.8 us (32%)
  blocking collectives  66.3 us (24%)
  waiting for transfers between devices  66.3 us (24%)
  starting transfers between devices  24.7 us (9%)
  between operations  15.2 us (5%)
  other arithmetic  14 us (5%)
    unnamed x2, waiting for transfers between devices  54.3 us
    scatter x1, local copies, waits for them, and re-layouts, on_device(): outgoing_grads = jnp.zeros((blocks, capacity, channels), jnp.bfloat16).at...  52.6 us
    scatter x1, local copies, waits for them, and re-layouts, on_device(): jnp.zeros((blocks, capacity), jnp.int32).at[owners, ranks].set(slots)  25.3 us
    all_gather x1, blocking collectives, on_device(): lax.all_gather(mm_stack, 'blk', axis=1, tiled=True)  22.1 us
    ppermute x15, starting transfers between devices, exchange_in_pairs(): part = lax.ppermute(part, axis, [(d, d ^ mask) for d in range(ways)])  21.1 us
    all_gather x1, blocking collectives, on_device(): portion = lax.all_gather(qm_stack, 'blk', axis=1, tiled=True)  18.8 us
    all_to_all x1, blocking collectives, on_device(): lax.all_to_all(outgoing, 'blk', split_axis=0, concat_axis=0, tiled=True)  15.5 us
    all_to_all x1, waiting for transfers between devices, on_device(): lax.all_to_all(outgoing_grads, 'blk', split_axis=0, concat_axis=0, tiled=...  9.25 us
  transfers between devices with their start and end apart: 17, of which 3 were waited for; matrix products, arithmetic and copies ran while one was open for 2% of the time, Pallas kernels for 0%

profile of v1, /device:TPU:0, one launch (start us, length us, event | category | flops | bytes accessed | tf_op | source)
XLA Modules:
  0.0 279.7 jit_solution(16354665460716005134)
XLA Ops:
  7.2 0.8 copy.35
  8.3 1.2 reduce-window.6
  9.8 0.8 copy.39
  11.0 25.3 %scatter_fusion = s32[16,64]{1,0:T(8,128)S(1)} fusion(s32[16,64]{1,0:T(8,128)S(1)} %broadcast.158.clone, s32[512]{0:T(512)S(1)} %bitcast.73, s32[512]{0:T(512)S(1)} %reshape.249), kind=kCustom, calls=%fused_computation.2 | custom fusion | bytes 10240 | tf_op jit(solution)/shard_map/scatter | solution.py:86
  36.4 0.5 collective-permute-start
  36.9 2.6 collective-permute-start.1
  39.6 1.8 collective-permute-start.3
  41.4 22.1 %all_gather.6 = f32[4,8192]{1,0:T(4,128)S(1)} all-gather(f32[4,512]{1,0:T(4,128)S(1)} %pad_maximum_fusion), channel_id=1, replica_groups=mesh['blk'=16,'rep'=2] {'blk'}, dimensions={1}, use_global_device_ids=true | all-gather | bytes 139264 | tf_op jit(solution)/shard_map/all_gather | solution.py:74
  63.5 5.4 %while.24 = (s32[]{:T(128)}, f32[128]{0:T(128)S(1)}, f32[3,128]{1,0:T(4,128)S(1)}, f32[16,4,512]{2,1,0:T(4,128)S(1)}, s32[]{:T(128)}, /*index=5*/s32[]{:T(128)}, s32[]{}) while((s32[]{:T(128)}, f32[128]{0:T(128)S(1)}, f32[3,128]{1,0:T(4,128)S(1)}, f32[16,4,512]{2,1,0:T(4,128)S(1)}, s32[]{:T(128)}, /*index=5*/s32[]{:T(128)}, ...), condition=%wide.region_3.4_spmd.clone, body=%wide.region_0.3_spmd.clone.sunk | while | flops 721028 | bytes 552567 | solution.py:44
  68.9 4.9 %psum.14 = f32[128]{0:T(128)S(1)} all-reduce(f32[128]{0:T(128)S(1)} %get-tuple-element.58), channel_id=1, replica_groups=mesh['blk'=16,'rep'=2] {'rep'}, use_global_device_ids=true, to_apply=%region_4.5 | all-reduce | flops 128 | bytes 1024 | tf_op jit(solution)/shard_map/psum | solution.py:75
  74.9 1.5 collective-permute-start.6
  76.5 3.9 %collective-permute-start.8 = (s32[1,64]{1,0:T(1,128)S(1)}, s32[1,64]{1,0:T(1,128)S(1)}, u32[]{:S(2)}, u32[]{:S(2)}) collective-permute-start(s32[1,64]{1,0:T(1,128)S(1)} %get-tuple-element.131), channel_id=1, source_target_pairs={{0,18},{2,16},{4,22},{6,20},{8,26},{10,24},{12,30},{14,28},{16,2},... | collective-permute-start | bytes 776 | tf_op jit(solution)/shard_map/ppermute | solution.py:21
  80.6 2.4 collective-permute-start.10
  83.0 0.4 collective-permute-start.11
  83.4 4.4 %collective-permute-start.12 = (s32[1,64]{1,0:T(1,128)S(1)}, s32[1,64]{1,0:T(1,128)S(1)}, u32[]{:S(2)}, u32[]{:S(2)}) collective-permute-start(s32[1,64]{1,0:T(1,128)S(1)} %get-tuple-element.127), channel_id=1, source_target_pairs={{0,26},{2,24},{4,30},{6,28},{8,18},{10,16},{12,22},{14,20},{16,10}... | collective-permute-start | bytes 776 | tf_op jit(solution)/shard_map/ppermute | solution.py:21
  88.1 3.2 %collective-permute-start.14 = (s32[1,64]{1,0:T(1,128)S(1)}, s32[1,64]{1,0:T(1,128)S(1)}, u32[]{:S(2)}, u32[]{:S(2)}) collective-permute-start(s32[1,64]{1,0:T(1,128)S(1)} %get-tuple-element.125), channel_id=1, source_target_pairs={{0,30},{2,28},{4,26},{6,24},{8,22},{10,20},{12,18},{14,16},{16,14}... | collective-permute-start | bytes 776 | tf_op jit(solution)/shard_map/ppermute | solution.py:21
  91.4 2.7 collective-permute-done.13
  94.3 3.2 %gather_fusion = bf16[1024,128]{1,0:T(8,128)(2,1)S(1)} fusion(bf16[128,128]{1,0:T(8,128)(2,1)S(1)} %fusion.8, s32[1024]{0:T(1024)S(1)} %broadcast_clamp_fusion), kind=kCustom, calls=%fused_computation | custom fusion | bytes 528384 | tf_op jit(solution)/shard_map/jit(_take)/gather | solution.py:88
  97.8 15.5 %all_to_all.10 = bf16[16,64,128]{2,1,0:T(8,128)(2,1)S(1)} all-to-all(bf16[16,64,128]{2,1,0:T(8,128)(2,1)S(1)} %broadcast_select_fusion.1), channel_id=1, replica_groups=mesh['blk'=16,'rep'=2] {'blk'}, dimensions={0} | all-to-all | bytes 524288 | tf_op jit(solution)/shard_map/all_to_all | solution.py:89
  113.4 3.2 %gather_fusion.1 = bf16[512,128]{1,0:T(8,128)(2,1)S(1)} fusion(bf16[16,64,128]{2,1,0:T(8,128)(2,1)S(1)} %all_to_all.10, s32[512]{0:T(512)S(1)} %bitcast.75), kind=kCustom, calls=%fused_computation.1 | custom fusion | bytes 266240 | tf_op jit(solution)/shard_map/gather | solution.py:90
  116.7 0.4 multiply_reduce_fusion.3
  117.1 0.2 fusion.15
  117.6 0.7 broadcast_in_dim.34
  118.4 52.6 %scatter_fusion.1 = bf16[16,64,128]{2,1,0:T(8,128)(2,1)} fusion(bf16[16,64,128]{2,1,0:T(8,128)(2,1)} %broadcast_in_dim.34, s32[512]{0:T(512)S(1)} %bitcast.74, bf16[512,128]{1,0:T(8,128)(2,1)S(1)} %bitcast.78), kind=kCustom, calls=%fused_computation.3 | custom fusion | bytes 397312 | tf_op jit(solution)/shard_map/scatter | solution.py:114
  170.9 3.5 %all-to-all-start.1 = ((bf16[16,64,128]{2,1,0:T(8,128)(2,1)}), bf16[16,64,128]{2,1,0:T(8,128)(2,1)S(1)}, u32[]{:S(2)}, u32[]{:S(2)}) async-start(bf16[16,64,128]{2,1,0:T(8,128)(2,1)} %scatter_fusion.1), calls=%async_computation.1 | async-start | bytes 524288 | tf_op jit(solution)/shard_map/all_to_all | solution.py:116
  174.7 0.5 multiply_add_fusion
  175.2 9.3 %all-to-all-done.1 = bf16[16,64,128]{2,1,0:T(8,128)(2,1)S(1)} async-done(((bf16[16,64,128]{2,1,0:T(8,128)(2,1)}), bf16[16,64,128]{2,1,0:T(8,128)(2,1)S(1)}, u32[]{:S(2)}, u32[]{:S(2)}) %all-to-all-start.1) | async-done | bytes 262176 | tf_op jit(solution)/shard_map/all_to_all | solution.py:116
  184.5 0.6 fusion.10
  185.1 18.8 %all_gather.7 = f32[4,2048]{1,0:T(4,128)S(1)} all-gather(f32[4,128]{1,0:T(4,128)S(1)} %pad_maximum_fusion.1), channel_id=1, replica_groups=mesh['blk'=16,'rep'=2] {'blk'}, dimensions={1}, use_global_device_ids=true | all-gather | bytes 34816 | tf_op jit(solution)/shard_map/all_gather | solution.py:129
  203.8 6.3 %while.25 = (s32[]{:T(128)}, f32[3,512]{1,0:T(4,128)S(1)}, f32[4,3,512]{2,1,0:T(4,128)S(1)}, f32[4,4,512]{2,1,0:T(4,128)S(1)}, f32[3,512]{1,0:T(4,128)S(1)}, /*index=5*/f32[512]{0:T(512)S(1)}, s32[]{:T(128)}, s32[]{:T(128)}, s32[]{}) while((s32[]{:T(128)}, f32[3,512]{1,0:T(4,128)S(1)}, f32[4,3,512]{2,1,0:T(4,128)S(1)}, ...), condition=%wide.region_18.19_spmd.clone, body=%wide.region_14.18_spmd.clone.sunk | while | flops 7341572 | bytes 6385803 | solution.py:139
  203.8 0.4 fusion.39
  204.2 0.2 broadcast_multiply_fusion.5
  204.4 0.9 fusion.40
  205.4 0.4 fusion.39
  205.8 0.2 broadcast_multiply_fusion.5
  206.0 0.9 fusion.40
  207.0 0.4 fusion.39
  207.4 0.2 broadcast_multiply_fusion.5
  207.6 0.9 fusion.40
  208.6 0.4 fusion.39
  209.0 0.2 broadcast_multiply_fusion.5
  209.2 0.9 fusion.40
  210.2 1.4 copy.44
  211.6 0.6 broadcast_multiply_fusion.1
  212.2 54.2 %reduce-scatter.4.cloned.1.call-done = f32[128,3]{1,0:T(8,128)} async-done(((f32[2048,3]{1,0:T(8,128)}), f32[128,3]{1,0:T(8,128)}) %reduce-scatter.4.cloned.1.call-update) | async-done | bytes 1552
  266.4 0.9 copy.45
  267.3 4.9 %psum.15 = f32[3,128]{1,0:T(4,128)S(1)} all-reduce(f32[3,128]{1,0:T(4,128)S(1)} %copy.45), channel_id=1, replica_groups=mesh['blk'=16,'rep'=2] {'rep'}, use_global_device_ids=true, to_apply=%region_20.21 | all-reduce | flops 384 | bytes 3072 | tf_op jit(solution)/shard_map/psum | solution.py:144
  272.3 0.6 broadcast_multiply_fusion.2
  (186 shorter events, 8.0 us)
Async XLA Ops:
  7.2 109.5 %copy-start = (bf16[128,256]{1,0:T(8,128)(2,1)S(1)}, bf16[128,256]{1,0:T(8,128)(2,1)}, u32[]{:S(2)}) copy-start(bf16[128,256]{1,0:T(8,128)(2,1)} %param.27) | copy-start | bytes 196612
  10.9 30.4 %copy-start.1 = (f32[3,512]{1,0:T(4,128)S(1)}, f32[3,512]{1,0:T(4,128)}, u32[]{:S(2)}) copy-start(f32[3,512]{1,0:T(4,128)} %param.22) | copy-start | bytes 18436
  11.0 30.4 %copy-start.3 = (f32[512]{0:T(512)S(1)}, f32[512]{0:T(512)}, u32[]{:S(2)}) copy-start(f32[512]{0:T(512)} %param.23) | copy-start | bytes 6148
  11.0 52.5 %copy-start.2 = (f32[3,128]{1,0:T(4,128)S(1)}, f32[3,128]{1,0:T(4,128)}, u32[]{:S(2)}) copy-start(f32[3,128]{1,0:T(4,128)} %param.17) | copy-start | bytes 4612
  36.4 38.4 %collective-permute-start = (s32[1,64]{1,0:T(1,128)S(1)}, s32[1,64]{1,0:T(1,128)S(1)}, u32[]{:S(2)}, u32[]{:S(2)}) collective-permute-start(s32[1,64]{1,0:T(1,128)S(1)} %get-tuple-element.139), channel_id=1, source_target_pairs={{0,2},{2,0},{4,6},{6,4},{8,10},{10,8},{12,14},{14,12},{16,18},{18,... | collective-permute-start | bytes 776 | tf_op jit(solution)/shard_map/ppermute | solution.py:21
  36.9 38.0 %collective-permute-start.1 = (s32[1,64]{1,0:T(1,128)S(1)}, s32[1,64]{1,0:T(1,128)S(1)}, u32[]{:S(2)}, u32[]{:S(2)}) collective-permute-start(s32[1,64]{1,0:T(1,128)S(1)} %get-tuple-element.138), channel_id=1, source_target_pairs={{0,4},{2,6},{4,0},{6,2},{8,12},{10,14},{12,8},{14,10},{16,20},{18,... | collective-permute-start | bytes 776 | tf_op jit(solution)/shard_map/ppermute | solution.py:21
  39.5 36.9 %collective-permute-start.2 = (s32[1,64]{1,0:T(1,128)S(1)}, s32[1,64]{1,0:T(1,128)S(1)}, u32[]{:S(2)}, u32[]{:S(2)}) collective-permute-start(s32[1,64]{1,0:T(1,128)S(1)} %get-tuple-element.137), channel_id=1, source_target_pairs={{0,6},{2,4},{4,2},{6,0},{8,14},{10,12},{12,10},{14,8},{16,22},{18,... | collective-permute-start | bytes 776 | tf_op jit(solution)/shard_map/ppermute | solution.py:21
  39.6 37.0 %collective-permute-start.3 = (s32[1,64]{1,0:T(1,128)S(1)}, s32[1,64]{1,0:T(1,128)S(1)}, u32[]{:S(2)}, u32[]{:S(2)}) collective-permute-start(s32[1,64]{1,0:T(1,128)S(1)} %get-tuple-element.136), channel_id=1, source_target_pairs={{0,8},{2,10},{4,12},{6,14},{8,0},{10,2},{12,4},{14,6},{16,24},{18,... | collective-permute-start | bytes 776 | tf_op jit(solution)/shard_map/ppermute | solution.py:21
  41.4 39.1 %collective-permute-start.4 = (s32[1,64]{1,0:T(1,128)S(1)}, s32[1,64]{1,0:T(1,128)S(1)}, u32[]{:S(2)}, u32[]{:S(2)}) collective-permute-start(s32[1,64]{1,0:T(1,128)S(1)} %get-tuple-element.135), channel_id=1, source_target_pairs={{0,10},{2,8},{4,14},{6,12},{8,2},{10,0},{12,6},{14,4},{16,26},{18,... | collective-permute-start | bytes 776 | tf_op jit(solution)/shard_map/ppermute | solution.py:21
  63.5 11.0 %copy-start.5 = (bf16[8,128]{1,0:T(8,128)(2,1)S(1)}, bf16[8,128]{1,0:T(8,128)(2,1)}, u32[]{:S(2)}) copy-start(bf16[8,128]{1,0:T(8,128)(2,1)} %param.24) | copy-start | bytes 6148
  63.5 11.0 %copy-start.8 = (s32[128]{0:T(128)S(1)}, s32[128]{0:T(128)}, u32[]{:S(2)}) copy-start(s32[128]{0:T(128)} %param.18) | copy-start | bytes 1540
  63.5 11.0 %copy-start.9 = (f32[128]{0:T(128)S(1)}, f32[128]{0:T(128)}, u32[]{:S(2)}) copy-start(f32[128]{0:T(128)} %param.25) | copy-start | bytes 1540
  74.8 5.8 %collective-permute-start.5 = (s32[1,64]{1,0:T(1,128)S(1)}, s32[1,64]{1,0:T(1,128)S(1)}, u32[]{:S(2)}, u32[]{:S(2)}) collective-permute-start(s32[1,64]{1,0:T(1,128)S(1)} %get-tuple-element.134), channel_id=1, source_target_pairs={{0,12},{2,14},{4,8},{6,10},{8,4},{10,6},{12,0},{14,2},{16,28},{18,... | collective-permute-start | bytes 776 | tf_op jit(solution)/shard_map/ppermute | solution.py:21
  74.9 8.1 %collective-permute-start.6 = (s32[1,64]{1,0:T(1,128)S(1)}, s32[1,64]{1,0:T(1,128)S(1)}, u32[]{:S(2)}, u32[]{:S(2)}) collective-permute-start(s32[1,64]{1,0:T(1,128)S(1)} %get-tuple-element.133), channel_id=1, source_target_pairs={{0,14},{2,12},{4,10},{6,8},{8,6},{10,4},{12,2},{14,0},{16,30},{18,... | collective-permute-start | bytes 776 | tf_op jit(solution)/shard_map/ppermute | solution.py:21
  76.4 7.0 %collective-permute-start.7 = (s32[1,64]{1,0:T(1,128)S(1)}, s32[1,64]{1,0:T(1,128)S(1)}, u32[]{:S(2)}, u32[]{:S(2)}) collective-permute-start(s32[1,64]{1,0:T(1,128)S(1)} %get-tuple-element.132), channel_id=1, source_target_pairs={{0,16},{2,18},{4,20},{6,22},{8,24},{10,26},{12,28},{14,30},{16,0},... | collective-permute-start | bytes 776 | tf_op jit(solution)/shard_map/ppermute | solution.py:21
  76.5 11.3 %collective-permute-start.8 = (s32[1,64]{1,0:T(1,128)S(1)}, s32[1,64]{1,0:T(1,128)S(1)}, u32[]{:S(2)}, u32[]{:S(2)}) collective-permute-start(s32[1,64]{1,0:T(1,128)S(1)} %get-tuple-element.131), channel_id=1, source_target_pairs={{0,18},{2,16},{4,22},{6,20},{8,26},{10,24},{12,30},{14,28},{16,2},... | collective-permute-start | bytes 776 | tf_op jit(solution)/shard_map/ppermute | solution.py:21
  80.4 7.6 %collective-permute-start.9 = (s32[1,64]{1,0:T(1,128)S(1)}, s32[1,64]{1,0:T(1,128)S(1)}, u32[]{:S(2)}, u32[]{:S(2)}) collective-permute-start(s32[1,64]{1,0:T(1,128)S(1)} %get-tuple-element.130), channel_id=1, source_target_pairs={{0,20},{2,22},{4,16},{6,18},{8,28},{10,30},{12,24},{14,26},{16,4},... | collective-permute-start | bytes 776 | tf_op jit(solution)/shard_map/ppermute | solution.py:21
  80.6 10.7 %collective-permute-start.10 = (s32[1,64]{1,0:T(1,128)S(1)}, s32[1,64]{1,0:T(1,128)S(1)}, u32[]{:S(2)}, u32[]{:S(2)}) collective-permute-start(s32[1,64]{1,0:T(1,128)S(1)} %get-tuple-element.129), channel_id=1, source_target_pairs={{0,22},{2,20},{4,18},{6,16},{8,30},{10,28},{12,26},{14,24},{16,6},... | collective-permute-start | bytes 776 | tf_op jit(solution)/shard_map/ppermute | solution.py:21
  83.0 8.4 %collective-permute-start.11 = (s32[1,64]{1,0:T(1,128)S(1)}, s32[1,64]{1,0:T(1,128)S(1)}, u32[]{:S(2)}, u32[]{:S(2)}) collective-permute-start(s32[1,64]{1,0:T(1,128)S(1)} %get-tuple-element.128), channel_id=1, source_target_pairs={{0,24},{2,26},{4,28},{6,30},{8,16},{10,18},{12,20},{14,22},{16,8},... | collective-permute-start | bytes 776 | tf_op jit(solution)/shard_map/ppermute | solution.py:21
  83.4 8.0 %collective-permute-start.12 = (s32[1,64]{1,0:T(1,128)S(1)}, s32[1,64]{1,0:T(1,128)S(1)}, u32[]{:S(2)}, u32[]{:S(2)}) collective-permute-start(s32[1,64]{1,0:T(1,128)S(1)} %get-tuple-element.127), channel_id=1, source_target_pairs={{0,26},{2,24},{4,30},{6,28},{8,18},{10,16},{12,22},{14,20},{16,10}... | collective-permute-start | bytes 776 | tf_op jit(solution)/shard_map/ppermute | solution.py:21
  87.9 6.3 %collective-permute-start.13 = (s32[1,64]{1,0:T(1,128)S(1)}, s32[1,64]{1,0:T(1,128)S(1)}, u32[]{:S(2)}, u32[]{:S(2)}) collective-permute-start(s32[1,64]{1,0:T(1,128)S(1)} %get-tuple-element.126), channel_id=1, source_target_pairs={{0,28},{2,30},{4,24},{6,26},{8,20},{10,22},{12,16},{14,18},{16,12}... | collective-permute-start | bytes 776 | tf_op jit(solution)/shard_map/ppermute | solution.py:21
  88.1 6.1 %collective-permute-start.14 = (s32[1,64]{1,0:T(1,128)S(1)}, s32[1,64]{1,0:T(1,128)S(1)}, u32[]{:S(2)}, u32[]{:S(2)}) collective-permute-start(s32[1,64]{1,0:T(1,128)S(1)} %get-tuple-element.125), channel_id=1, source_target_pairs={{0,30},{2,28},{4,26},{6,24},{8,22},{10,20},{12,18},{14,16},{16,14}... | collective-permute-start | bytes 776 | tf_op jit(solution)/shard_map/ppermute | solution.py:21
  97.8 18.9 %copy-start.4 = (bf16[128,128]{1,0:T(8,128)(2,1)S(1)}, bf16[128,128]{1,0:T(8,128)(2,1)}, u32[]{:S(2)}) copy-start(bf16[128,128]{1,0:T(8,128)(2,1)} %param.26) | copy-start | bytes 98308
  97.8 18.9 %copy-start.6 = (f32[256]{0:T(256)S(1)}, f32[256]{0:T(256)}, u32[]{:S(2)}) copy-start(f32[256]{0:T(256)} %param.28) | copy-start | bytes 3076
  97.8 18.9 %copy-start.7 = (f32[256]{0:T(256)S(1)}, f32[256]{0:T(256)}, u32[]{:S(2)}) copy-start(f32[256]{0:T(256)} %param.29) | copy-start | bytes 3076
  170.9 13.5 %all-to-all-start.1 = ((bf16[16,64,128]{2,1,0:T(8,128)(2,1)}), bf16[16,64,128]{2,1,0:T(8,128)(2,1)S(1)}, u32[]{:S(2)}, u32[]{:S(2)}) async-start(bf16[16,64,128]{2,1,0:T(8,128)(2,1)} %scatter_fusion.1), calls=%async_computation.1 | async-start | bytes 524288 | tf_op jit(solution)/shard_map/all_to_all | solution.py:116
  174.5 92.0 %reduce-scatter.4.cloned.1.call-start = ((), (), s32[]{:S(2)}) async-start(), calls=%async_computation.3 | async-start | bytes 1114112
Sparse Core Ops, SparseCore 0:
  211.7 54.6 reduce-scatter.3
